TPU v7x, 32 devices: a whole 2x2x4 slice. The times are simulated.
32 devices in a mesh: basin: 8 (over z, y), band: 4 (over x, core).
Axes of the slice: x: 2, y: 2, z: 4, core: 2. Of those that a mesh axis runs over, the one named last changes fastest.
Arguments:
- precip: float32 [6144, 8, 128], P(('basin', 'band')), may hold values from 0.002 to 0.02
- soil_water: float32 [6144, 128], P(('basin', 'band')), may hold values from 0.1 to 1
- capacity: float32 [6144, 128], P(('basin', 'band')), may hold values from 0.1 to 1
- evap_rate: float32 [6144, 128], P(('basin', 'band')), may hold values from 0.01 to 0.1
- tile_dest: int32 [6144], P(('basin', 'band')), may hold values from 0 to 31, as said below
- tile_block: int32 [6144], P(('basin', 'band')), may hold values from 0 to 7
- trib_op: float32 [256, 128, 128], P(('basin', 'band')), may hold values from 0 to 1
- trib_keep: float32 [256, 128], P(('basin', 'band')), may hold values from 0.01 to 0.6
- trib_prev: float32 [256, 128], P(('basin', 'band')), may hold values from 0 to 0.5
- trib_river: int32 [256], P(('basin', 'band')), may hold values from 0 to 3, as said below
- trib_reach: int32 [256], P(('basin', 'band')), may hold values from 0 to 127
- main_op: float32 [4, 8, 128, 128], P('band', 'basin'), may hold values from 0 to 1
- main_keep: float32 [4, 8, 128], P('band', 'basin'), may hold values from 0.002 to 0.1
- main_prev: float32 [4, 8, 128], P('band', 'basin'), may hold values from 0 to 4
- head_inflow: float32 [4, 8], P('band'), may hold values from 0.5 to 2
Outputs:
- soil_final: float32 [6144, 128], P(('basin', 'band'))
- trib_final: float32 [256, 128], P(('basin', 'band'))
- main_flow: float32 [4, 8, 8, 128], P('band', 'basin')
Inputs may be any that keep to these rules, and one draw needn't show every extreme that they name: `tile_dest`: among the 192 tiles of one device, at most 12 name the same owner. `trib_river`: among the 8 tributary blocks of one device, at most 4 name the same river.
All inputs are finite; a program needn't handle non-finite values.
Results may differ from a plain program's by a relative error of at most 0.00016.
Values sent between devices are 32-bit elements; how exact they have to be, the bound alone decides.
No kernel may reach another device: no remote copies, remote signals or barrier semaphores. Data moves between devices by JAX's collectives and lax.ppermute only.
A program may use at most 64 MiB of HBM per device.

v0:
```python
import jax
import jax.numpy as jnp
from jax import lax
from jax.sharding import PartitionSpec as P


def entering(value, axis, join, neutral):
    count, mine = (lax.axis_size(axis), lax.axis_index(axis))
    pieces = jax.tree.map(lambda part: lax.all_gather(part, axis), value)
    running = jax.tree.map(
        lambda part, zero: jnp.full_like(part, 0) + jnp.asarray(zero, part.dtype), value, neutral
    )

    def turn(position, running):
        longer = join(running, jax.tree.map(lambda part: part[position], pieces))
        return jax.tree.map(lambda new, old: jnp.where(position < mine, new, old), longer, running)

    return lax.fori_loop(0, count - 1, turn, running)


def land_update(precip, soil_water, capacity, evap_rate):
    water = soil_water
    runoff_steps = []
    for sub_step in range(precip.shape[1]):
        rain_now = precip[:, sub_step]
        runoff_now = rain_now * water / (water + capacity)
        water = (1.0 - evap_rate) * water + rain_now - runoff_now
        runoff_steps.append(runoff_now)
    return (jnp.stack(runoff_steps, axis=1), water)


def route_series(mixed, keep, previous):
    flow = previous
    flows = []
    for sub_step in range(mixed.shape[-2]):
        flow = keep * flow + (1.0 - keep) * mixed[..., sub_step, :]
        flows.append(flow)
    return jnp.stack(flows, axis=-2)


def pack_slots(values, labels, targets, peer_count, slot_cap):
    entries = targets.shape[0]
    position = jnp.arange(entries, dtype=jnp.int32)
    earlier = (targets[:, None] == targets[None, :]) & (position[None, :] < position[:, None])
    ranking = jnp.sum(earlier.astype(jnp.int32), axis=1)
    target_slot = targets * slot_cap + ranking
    buffer = (
        jnp.zeros((peer_count * slot_cap, values.shape[1]), values.dtype)
        .at[target_slot]
        .set(values)
    )
    slot_labels = jnp.zeros((peer_count * slot_cap,), jnp.int32).at[target_slot].set(labels)
    return (buffer, slot_labels)


def compose(earlier, later):
    new_map = jnp.dot(later[0], earlier[0], precision=lax.Precision.HIGHEST)
    new_shift = jnp.dot(later[0], earlier[1], precision=lax.Precision.HIGHEST) + later[1]
    return (new_map, new_shift)


def local(
    precip,
    soil_water,
    capacity,
    evap_rate,
    tile_dest,
    tile_block,
    trib_op,
    trib_keep,
    trib_prev,
    trib_river,
    trib_reach,
    main_op,
    main_keep,
    main_prev,
    head_inflow,
):
    tile_count = precip.shape[0]
    sub_steps = precip.shape[1]
    reaches = precip.shape[2]
    blocks = trib_op.shape[0]
    chains = lax.axis_size("basin")
    rivers = lax.axis_size("band")
    shards = chains * rivers
    operator = main_op[0, 0]
    keep_main = main_keep[0, 0]
    decay = keep_main[reaches - 1]
    through = operator[reaches - 1, 0]
    transfer = jnp.zeros((sub_steps, sub_steps), jnp.float32)
    power = jnp.ones((), jnp.float32)
    for lag in range(sub_steps):
        transfer = transfer + power * jnp.eye(sub_steps, k=-lag, dtype=jnp.float32)
        power = power * decay
    transfer = transfer * (through * (1.0 - decay))
    runoff, water = land_update(precip, soil_water, capacity, evap_rate)
    tile_cap = max(2, 2 * tile_count // shards)
    buffer, slot_labels = pack_slots(
        runoff.reshape(tile_count, sub_steps * reaches), tile_block, tile_dest, shards, tile_cap
    )
    buffer = buffer.reshape(chains, rivers, tile_cap, sub_steps * reaches)
    slot_labels = slot_labels.reshape(chains, rivers, tile_cap)
    arrived, arrived_ids = (
        lax.all_to_all(
            lax.all_to_all(buffer, "basin", split_axis=0, concat_axis=0, tiled=True),
            "band",
            split_axis=1,
            concat_axis=1,
            tiled=True,
        ),
        lax.all_to_all(
            lax.all_to_all(slot_labels, "basin", split_axis=0, concat_axis=0, tiled=True),
            "band",
            split_axis=1,
            concat_axis=1,
            tiled=True,
        ),
    )
    received = arrived.reshape(-1, sub_steps * reaches)
    block_pick = (
        arrived_ids.reshape(-1)[:, None] == jnp.arange(blocks, dtype=jnp.int32)[None, :]
    ).astype(jnp.float32)
    lateral = jnp.einsum("sk,sx->kx", block_pick, received, precision=lax.Precision.HIGHEST)
    trib_mixed = jnp.einsum(
        "brc,btc->btr",
        trib_op,
        lateral.reshape(blocks, sub_steps, reaches),
        precision=lax.Precision.HIGHEST,
    )
    trib_flows = route_series(trib_mixed, trib_keep, trib_prev)
    outlet = trib_flows[:, :, reaches - 1]
    branch_cap = max(2, 2 * blocks // rivers)
    sent, sent_reach = pack_slots(outlet, trib_reach, trib_river, rivers, branch_cap)
    got, got_reach = (
        lax.all_to_all(
            sent.reshape(rivers, branch_cap, sub_steps),
            "band",
            split_axis=0,
            concat_axis=0,
            tiled=True,
        ),
        lax.all_to_all(
            sent_reach.reshape(rivers, branch_cap), "band", split_axis=0, concat_axis=0, tiled=True
        ),
    )
    reach_pick = (
        got_reach.reshape(-1)[:, None] == jnp.arange(reaches, dtype=jnp.int32)[None, :]
    ).astype(jnp.float32)
    branch_in = jnp.einsum(
        "sr,st->tr", reach_pick, got.reshape(-1, sub_steps), precision=lax.Precision.HIGHEST
    )
    main_mixed = jnp.einsum("rc,tc->tr", operator, branch_in, precision=lax.Precision.HIGHEST)
    base_flows = route_series(main_mixed, keep_main, main_prev[0, 0])
    own_exit = base_flows[:, reaches - 1]
    unit_map = jnp.eye(sub_steps, dtype=jnp.float32)
    no_shift = jnp.zeros((sub_steps,), jnp.float32)
    prefix_map, prefix_shift = entering(
        (transfer, own_exit), "basin", compose, (unit_map, no_shift)
    )
    entry = jnp.dot(prefix_map, head_inflow[0], precision=lax.Precision.HIGHEST) + prefix_shift
    fed_mixed = main_mixed + entry[:, None] * operator[:, 0][None, :]
    main_flows = route_series(fed_mixed, keep_main, main_prev[0, 0])
    return (water, trib_flows[:, sub_steps - 1], main_flows[None, None])


def solution(mesh):
    return jax.shard_map(
        local,
        mesh=mesh,
        in_specs=(
            P(("basin", "band"), None, None),
            P(("basin", "band"), None),
            P(("basin", "band"), None),
            P(("basin", "band"), None),
            P(("basin", "band")),
            P(("basin", "band")),
            P(("basin", "band"), None, None),
            P(("basin", "band"), None),
            P(("basin", "band"), None),
            P(("basin", "band")),
            P(("basin", "band")),
            P("band", "basin", None, None),
            P("band", "basin", None),
            P("band", "basin", None),
            P("band", None),
        ),
        out_specs=(
            P(("basin", "band"), None),
            P(("basin", "band"), None),
            P("band", "basin", None, None),
        ),
        check_vma=False,
    )
```

profile of v0, /device:TPU:0, one launch (start us, length us, event | category | flops | bytes accessed | tf_op | source)
XLA Modules:
  0.0 160.7 jit_solution(4654353818864081058)
XLA Ops:
  0.7 0.9 convert_reduce_fusion
  2.3 1.3 scatter_custom_fusion
  4.4 7.3 %all-to-all-start = ((s32[8,4,12]{2,1,0:T(4,128)}), s32[8,4,12]{2,1,0:T(4,128)S(1)}, u32[]{:S(2)}, u32[]{:S(2)}) async-start(s32[8,4,12]{2,1,0:T(4,128)} %reshape.312), calls=%async_computation | async-start | bytes 32768 | tf_op jit(solution)/shard_map/all_to_all | solution.py:112
  11.7 4.1 %fusion.63 = (f32[192,1,128]{2,1,0:T(1,128)S(1)}, f32[192,1,128]{2,1,0:T(1,128)S(1)}, f32[192,1,128]{2,1,0:T(1,128)S(1)}, f32[192,1,128]{2,1,0:T(1,128)S(1)}, f3...) fusion(f32[192,8,128]{2,1,0:T(8,128)} %param.17), kind=kLoop, calls=%fused_computation.144 | loop fusion | bytes 1572864 | tf_op jit(solution)/shard_map/slice | solution.py:25
  16.4 2.5 %scatter_custom_fusion.1 = f32[384,1024]{1,0:T(8,128)} fusion(s32[192]{0:T(256)S(1)} %compare_select_fusion, f32[8,24,8,128]{3,2,1,0:T(8,128)S(1)} %bitcast.264, f32[]{:T(128)} %constant.60.clone.1), kind=kCustom, calls=%fused_computation.20 | custom fusion | bytes 2359300 | tf_op jit(solution)/shard_map/scatter | solution.py:50
  18.9 1.4 reshape.314
  20.3 2.2 %copy.110 = f32[8,4,12,1024]{3,1,2,0:T(4,128)} copy(f32[8,4,12,1024]{3,2,1,0:T(8,128)S(1)} %reshape.314) | data formatting | bytes 3145728 | tf_op jit(solution)/shard_map/reshape | solution.py:101
  22.5 6.1 %all-to-all-start.2 = ((f32[8,4,12,1024]{3,1,2,0:T(4,128)}), f32[8,4,12,1024]{3,1,2,0:T(4,128)S(1)}, u32[]{:S(2)}, u32[]{:S(2)}) async-start(f32[8,4,12,1024]{3,1,2,0:T(4,128)} %copy.110), calls=%async_computation.2 | async-start | bytes 3145728 | tf_op jit(solution)/shard_map/all_to_all | solution.py:105
  29.3 35.8 %all-to-all-done.2 = f32[8,4,12,1024]{3,1,2,0:T(4,128)S(1)} async-done(((f32[8,4,12,1024]{3,1,2,0:T(4,128)}), f32[8,4,12,1024]{3,1,2,0:T(4,128)S(1)}, u32[]{:S(2)}, u32[]{:S(2)}) %all-to-all-start.2) | async-done | bytes 1572896 | tf_op jit(solution)/shard_map/all_to_all | solution.py:105
  65.1 3.3 %all-to-all-start.1 = ((s32[8,4,12]{2,0,1:T(8,128)}), s32[8,4,12]{2,0,1:T(8,128)S(1)}, u32[]{:S(2)}, u32[]{:S(2)}) async-start(s32[8,4,12]{2,0,1:T(8,128)} %copy.107), calls=%async_computation.1 | async-start | bytes 32768 | tf_op jit(solution)/shard_map/all_to_all | solution.py:111
  68.6 2.1 %copy.111 = f32[8,4,12,1024]{3,0,2,1:T(8,128)} copy(f32[8,4,12,1024]{3,1,2,0:T(4,128)S(1)} %all-to-all-done.2) | data formatting | bytes 3145728 | tf_op jit(solution)/shard_map/all_to_all | solution.py:105
  70.6 1.5 all-to-all-done.1
  72.2 3.6 %all-to-all-start.3 = ((f32[8,4,12,1024]{3,0,2,1:T(8,128)}), f32[8,4,12,1024]{3,0,2,1:T(8,128)S(1)}, u32[]{:S(2)}, u32[]{:S(2)}) async-start(f32[8,4,12,1024]{3,0,2,1:T(8,128)} %copy.111), calls=%async_computation.3 | async-start | bytes 3145728 | tf_op jit(solution)/shard_map/all_to_all | solution.py:104
  84.9 30.4 %all_gather.7 = f32[8,8,8]{2,1,0:T(8,128)S(1)} all-gather(f32[1,8,8]{2,1,0:T(8,128)S(1)} %add_multiply_fusion), channel_id=1, replica_groups=mesh['basin'=8,'band'=4] {'basin'}, dimensions={0}, use_global_device_ids=true | all-gather | bytes 2304 | tf_op jit(solution)/shard_map/all_gather | solution.py:9
  116.3 1.2 copy-done.2
  117.4 3.2 %all-to-all-start.5 = ((s32[4,1,4]{2,1,0:T(1,128)}), s32[4,1,4]{2,1,0:T(1,128)S(1)}, u32[]{:S(2)}, u32[]{:S(2)}) async-start(s32[4,1,4]{2,1,0:T(1,128)} %bitcast.40), calls=%async_computation.5 | async-start | bytes 4096 | tf_op jit(solution)/shard_map/all_to_all | solution.py:142
  120.7 2.4 %copy.112 = f32[8,4,12,1024]{3,2,1,0:T(8,128)S(1)} copy(f32[8,4,12,1024]{3,0,2,1:T(8,128)} %copy-done.2) | data formatting | bytes 3145728 | tf_op jit(solution)/shard_map/all_to_all | solution.py:104
  123.0 1.3 reshape.315
  124.4 1.9 %copy.113 = f32[1024,384]{1,0:T(8,128)S(1)} copy(f32[1024,384]{0,1:T(8,128)} %bitcast.246) | data formatting | bytes 3145728 | tf_op jit(solution)/shard_map/sk,sx->kx/dot_general | solution.py:123
  129.0 1.2 scatter_custom_fusion.2
  130.2 3.3 %all-to-all-start.4 = ((f32[4,4,8]{2,1,0:T(4,128)}), f32[4,4,8]{2,1,0:T(4,128)S(1)}, u32[]{:S(2)}, u32[]{:S(2)}) async-start(f32[4,4,8]{2,1,0:T(4,128)} %bitcast.38), calls=%async_computation.4 | async-start | bytes 16384 | tf_op jit(solution)/shard_map/all_to_all | solution.py:135
  136.0 1.3 all-to-all-done.4
  138.2 19.5 %all-reduce = f32[64]{0:T(128)S(1)} all-reduce(f32[64]{0:T(128)S(1)} %dynamic-update-slice), channel_id=2, replica_groups=mesh['basin'=8,'band'=4] {'basin'}, use_global_device_ids=true, to_apply=%add | all-reduce | flops 64 | bytes 512
  157.8 2.0 %while.16 = (s32[]{:T(128)}, f32[8,8]{1,0:T(8,128)S(1)}, f32[8]{0:T(128)S(1)}, s32[]{:T(128)}, f32[8,8,8]{2,1,0:T(8,128)S(1)}, /*index=5*/f32[8,8]{1,0:T(8,128)S(1)}, s32[]{:T(128)}, s32[]{:T(128)}) while((s32[]{:T(128)}, f32[8,8]{1,0:T(8,128)S(1)}, f32[8]{0:T(128)S(1)}, s32[]{:T(128)}, f32[8,8,8]{2,1,0:T(8,128)S(1)}, ...), condition=%wide.region_7.8_spmd.clone, body=%wide.region_6.7_spmd.clone.sunk | while | flops 7012 | bytes 21460 | solution.py:18
  (113 shorter events, 15.3 us)
Async XLA Ops:
  0.6 126.5 %copy-start = (f32[8,128,128]{2,1,0:T(8,128)S(1)}, f32[8,128,128]{2,1,0:T(8,128)}, u32[]{:S(2)}) copy-start(f32[8,128,128]{2,1,0:T(8,128)} %param.23) | copy-start | bytes 1572868
  0.6 15.2 %copy-start.1 = (f32[192,128]{1,0:T(8,128)S(1)}, f32[192,128]{1,0:T(8,128)}, u32[]{:S(2)}) copy-start(f32[192,128]{1,0:T(8,128)} %param.19) | copy-start | bytes 294916
  0.7 15.2 %copy-start.4 = (f32[192,128]{1,0:T(8,128)S(1)}, f32[192,128]{1,0:T(8,128)}, u32[]{:S(2)}) copy-start(f32[192,128]{1,0:T(8,128)} %param.18) | copy-start | bytes 294916
  0.7 15.2 %copy-start.3 = (f32[192,128]{1,0:T(8,128)S(1)}, f32[192,128]{1,0:T(8,128)}, u32[]{:S(2)}) copy-start(f32[192,128]{1,0:T(8,128)} %param.20) | copy-start | bytes 294916
  4.4 18.1 %all-to-all-start = ((s32[8,4,12]{2,1,0:T(4,128)}), s32[8,4,12]{2,1,0:T(4,128)S(1)}, u32[]{:S(2)}, u32[]{:S(2)}) async-start(s32[8,4,12]{2,1,0:T(4,128)} %reshape.312), calls=%async_computation | async-start | bytes 32768 | tf_op jit(solution)/shard_map/all_to_all | solution.py:112
  22.5 45.8 %copy-start.10 = (s32[8]{0:T(128)S(1)}, s32[8]{0:T(128)}, u32[]{:S(2)}) copy-start(s32[8]{0:T(128)} %param.26) | copy-start | bytes 100
  22.5 42.6 %all-to-all-start.2 = ((f32[8,4,12,1024]{3,1,2,0:T(4,128)}), f32[8,4,12,1024]{3,1,2,0:T(4,128)S(1)}, u32[]{:S(2)}, u32[]{:S(2)}) async-start(f32[8,4,12,1024]{3,1,2,0:T(4,128)} %copy.110), calls=%async_computation.2 | async-start | bytes 3145728 | tf_op jit(solution)/shard_map/all_to_all | solution.py:105
  65.1 7.1 %all-to-all-start.1 = ((s32[8,4,12]{2,0,1:T(8,128)}), s32[8,4,12]{2,0,1:T(8,128)S(1)}, u32[]{:S(2)}, u32[]{:S(2)}) async-start(s32[8,4,12]{2,0,1:T(8,128)} %copy.107), calls=%async_computation.1 | async-start | bytes 32768 | tf_op jit(solution)/shard_map/all_to_all | solution.py:111
  70.6 6.6 %copy-start.5 = (f32[1,1,128,128]{3,2,1,0:T(8,128)S(1)}, f32[1,1,128,128]{3,2,1,0:T(8,128)}, u32[]{:S(2)}) copy-start(f32[1,1,128,128]{3,2,1,0:T(8,128)} %param.28) | copy-start | bytes 196612
  70.6 7.1 %copy-start.8 = (f32[1,1,128]{2,1,0:T(1,128)S(1)}, f32[1,1,128]{2,1,0:T(1,128)}, u32[]{:S(2)}) copy-start(f32[1,1,128]{2,1,0:T(1,128)} %param.29) | copy-start | bytes 1540
  72.2 44.1 %all-to-all-start.3 = ((f32[8,4,12,1024]{3,0,2,1:T(8,128)}), f32[8,4,12,1024]{3,0,2,1:T(8,128)S(1)}, u32[]{:S(2)}, u32[]{:S(2)}) async-start(f32[8,4,12,1024]{3,0,2,1:T(8,128)} %copy.111), calls=%async_computation.3 | async-start | bytes 3145728 | tf_op jit(solution)/shard_map/all_to_all | solution.py:104
  116.3 1.2 copy-start.2
  117.4 12.8 %all-to-all-start.5 = ((s32[4,1,4]{2,1,0:T(1,128)}), s32[4,1,4]{2,1,0:T(1,128)S(1)}, u32[]{:S(2)}, u32[]{:S(2)}) async-start(s32[4,1,4]{2,1,0:T(1,128)} %bitcast.40), calls=%async_computation.5 | async-start | bytes 4096 | tf_op jit(solution)/shard_map/all_to_all | solution.py:142
  126.2 1.9 %copy-start.6 = (f32[8,128]{1,0:T(8,128)S(1)}, f32[8,128]{1,0:T(8,128)}, u32[]{:S(2)}) copy-start(f32[8,128]{1,0:T(8,128)} %param.24) | copy-start | bytes 12292
  126.2 1.9 %copy-start.7 = (f32[8,128]{1,0:T(8,128)S(1)}, f32[8,128]{1,0:T(8,128)}, u32[]{:S(2)}) copy-start(f32[8,128]{1,0:T(8,128)} %param.25) | copy-start | bytes 12292
  126.3 7.2 %copy-start.12 = (u32[32]{0:T(128)S(1)}, u32[32]{0:T(128)}, u32[]{:S(2)}) copy-start(u32[32]{0:T(128)} %constant.83) | copy-start | bytes 388
  126.3 11.4 %copy-start.9 = (f32[1,1,128]{2,1,0:T(1,128)S(1)}, f32[1,1,128]{2,1,0:T(1,128)}, u32[]{:S(2)}) copy-start(f32[1,1,128]{2,1,0:T(1,128)} %param.30) | copy-start | bytes 1540
  126.3 33.5 %copy-start.11 = (f32[1,8]{1,0:T(1,128)S(1)}, f32[1,8]{1,0:T(1,128)}, u32[]{:S(2)}) copy-start(f32[1,8]{1,0:T(1,128)} %param.31) | copy-start | bytes 100
  130.2 7.1 %all-to-all-start.4 = ((f32[4,4,8]{2,1,0:T(4,128)}), f32[4,4,8]{2,1,0:T(4,128)S(1)}, u32[]{:S(2)}, u32[]{:S(2)}) async-start(f32[4,4,8]{2,1,0:T(4,128)} %bitcast.38), calls=%async_computation.4 | async-start | bytes 16384 | tf_op jit(solution)/shard_map/all_to_all | solution.py:135
where the time goes:
time: 161 us
  blocking collectives  49.9 us (31%)
  waiting for transfers between devices  38.7 us (24%)
  local copies, waits for them, and re-layouts  28.2 us (18%)
  starting transfers between devices  26.7 us (17%)
  between operations  7.51 us (5%)
  other arithmetic  5.32 us (3%)
  matrix products  4.27 us (3%)
    all_to_all x1, waiting for transfers between devices, local(): lax.all_to_all(buffer, 'basin', split_axis=0, concat_axis=0, tiled=True)  35.8 us
    all_gather x1, blocking collectives, entering(): pieces = jax.tree.map(lambda part: lax.all_gather(part, axis), value)  30.4 us
    unnamed x1, blocking collectives  19.5 us
    all_to_all x1, starting transfers between devices, local(): lax.all_to_all(slot_labels, 'basin', split_axis=0, concat_axis=0, tiled=T...  7.28 us
    all_to_all x1, starting transfers between devices, local(): lax.all_to_all(buffer, 'basin', split_axis=0, concat_axis=0, tiled=True)  6.13 us
    slice x1, local copies, waits for them, and re-layouts, land_update(): rain_now = precip[:, sub_step]  4.11 us
    scatter x2, local copies, waits for them, and re-layouts, pack_slots(): buffer = jnp.zeros((peer_count * slot_cap, values.shape[1]), values.dtype...  3.65 us
    reshape x2, local copies, waits for them, and re-layouts, local(): buffer = buffer.reshape(chains, rivers, tile_cap, sub_steps * reaches)  3.63 us
  transfers between devices with their start and end apart: 6, of which 3 were waited for; matrix products, arithmetic and copies ran while one was open for 18% of the time, Pallas kernels for 0%

commit v1 on v0

--- a/solution.py
+++ b/solution.py
@@ -2,6 +2,7 @@
 import jax.numpy as jnp
 from jax import lax
 from jax.sharding import PartitionSpec as P
+from jax.lax import all_to_all, axis_size
 
 
 def entering(value, axis, join, neutral):
@@ -108,12 +109,23 @@
             concat_axis=1,
             tiled=True,
         ),
-        lax.all_to_all(
-            lax.all_to_all(slot_labels, "basin", split_axis=0, concat_axis=0, tiled=True),
-            "band",
-            split_axis=1,
-            concat_axis=1,
-            tiled=True,
+        jnp.concatenate(
+            all_to_all(
+                jnp.stack(
+                    jnp.split(
+                        lax.all_to_all(
+                            slot_labels, "basin", split_axis=0, concat_axis=0, tiled=True
+                        ),
+                        axis_size("band"),
+                        1,
+                    ),
+                    axis=0,
+                ),
+                "band",
+                0,
+                0,
+            ),
+            axis=1,
         ),
     )
     received = arrived.reshape(-1, sub_steps * reaches)

time: 161 us -> 161 us (level)
  no operation moved by 1% of the time
where the time goes in v1:
time: 161 us
  blocking collectives  49.9 us (31%)
  waiting for transfers between devices  38.7 us (24%)
  local copies, waits for them, and re-layouts  27.7 us (17%)
  starting transfers between devices  26.7 us (17%)
  between operations  7.51 us (5%)
  other arithmetic  5.93 us (4%)
  matrix products  4.27 us (3%)
    all_to_all x1, waiting for transfers between devices, local(): lax.all_to_all(buffer, 'basin', split_axis=0, concat_axis=0, tiled=True)  35.8 us
    all_gather x1, blocking collectives, entering(): pieces = jax.tree.map(lambda part: lax.all_gather(part, axis), value)  30.4 us
    unnamed x1, blocking collectives  19.5 us
    all_to_all x1, starting transfers between devices, local(): lax.all_to_all(slot_labels, 'basin', split_axis=0, concat_axis=0, tiled=T...  7.28 us
    all_to_all x1, starting transfers between devices, local(): lax.all_to_all(buffer, 'basin', split_axis=0, concat_axis=0, tiled=True)  6.13 us
    slice x1, local copies, waits for them, and re-layouts, land_update(): rain_now = precip[:, sub_step]  4.11 us
    scatter x2, local copies, waits for them, and re-layouts, pack_slots(): buffer = jnp.zeros((peer_count * slot_cap, values.shape[1]), values.dtype...  3.66 us
    reshape x2, local copies, waits for them, and re-layouts, local(): buffer = buffer.reshape(chains, rivers, tile_cap, sub_steps * reaches)  3.64 us
  transfers between devices with their start and end apart: 6, of which 3 were waited for; matrix products, arithmetic and copies ran while one was open for 18% of the time, Pallas kernels for 0%

profile of v1, /device:TPU:0, one launch (start us, length us, event | category | flops | bytes accessed | tf_op | source)
XLA Modules:
  0.0 160.7 jit_solution(16681314854573507074)
XLA Ops:
  0.7 0.9 convert_reduce_fusion
  2.3 1.3 scatter_custom_fusion
  4.4 7.3 %all-to-all-start = ((s32[8,4,12]{2,1,0:T(4,128)}), s32[8,4,12]{2,1,0:T(4,128)S(1)}, u32[]{:S(2)}, u32[]{:S(2)}) async-start(s32[8,4,12]{2,1,0:T(4,128)} %reshape.315), calls=%async_computation | async-start | bytes 32768 | tf_op jit(solution)/shard_map/all_to_all | solution.py:116
  11.7 4.1 %fusion.63 = (f32[192,1,128]{2,1,0:T(1,128)S(1)}, f32[192,1,128]{2,1,0:T(1,128)S(1)}, f32[192,1,128]{2,1,0:T(1,128)S(1)}, f32[192,1,128]{2,1,0:T(1,128)S(1)}, f3...) fusion(f32[192,8,128]{2,1,0:T(8,128)} %param.17), kind=kLoop, calls=%fused_computation.145 | loop fusion | bytes 1572864 | tf_op jit(solution)/shard_map/slice | solution.py:26
  16.4 2.5 %scatter_custom_fusion.1 = f32[384,1024]{1,0:T(8,128)} fusion(s32[192]{0:T(256)S(1)} %compare_select_fusion, f32[8,24,8,128]{3,2,1,0:T(8,128)S(1)} %bitcast.271, f32[]{:T(128)} %constant.60.clone.1), kind=kCustom, calls=%fused_computation.20 | custom fusion | bytes 2359300 | tf_op jit(solution)/shard_map/scatter | solution.py:51
  18.9 1.4 reshape.318
  20.3 2.2 %copy.86 = f32[8,4,12,1024]{3,1,2,0:T(4,128)} copy(f32[8,4,12,1024]{3,2,1,0:T(8,128)S(1)} %reshape.318) | data formatting | bytes 3145728 | tf_op jit(solution)/shard_map/reshape | solution.py:102
  22.5 6.1 %all-to-all-start.2 = ((f32[8,4,12,1024]{3,1,2,0:T(4,128)}), f32[8,4,12,1024]{3,1,2,0:T(4,128)S(1)}, u32[]{:S(2)}, u32[]{:S(2)}) async-start(f32[8,4,12,1024]{3,1,2,0:T(4,128)} %copy.86), calls=%async_computation.2 | async-start | bytes 3145728 | tf_op jit(solution)/shard_map/all_to_all | solution.py:106
  29.3 35.8 %all-to-all-done.2 = f32[8,4,12,1024]{3,1,2,0:T(4,128)S(1)} async-done(((f32[8,4,12,1024]{3,1,2,0:T(4,128)}), f32[8,4,12,1024]{3,1,2,0:T(4,128)S(1)}, u32[]{:S(2)}, u32[]{:S(2)}) %all-to-all-start.2) | async-done | bytes 1572896 | tf_op jit(solution)/shard_map/all_to_all | solution.py:106
  65.1 3.3 %all-to-all-start.1 = ((s32[4,8,1,12]{3,1,2,0:T(8,128)}), s32[4,8,1,12]{3,1,2,0:T(8,128)S(1)}, u32[]{:S(2)}, u32[]{:S(2)}) async-start(s32[4,8,1,12]{3,1,2,0:T(8,128)} %pad_add_fusion), calls=%async_computation.1 | async-start | bytes 32768 | tf_op jit(solution)/shard_map/all_to_all | solution.py:113
  68.6 2.1 %copy.87 = f32[8,4,12,1024]{3,0,2,1:T(8,128)} copy(f32[8,4,12,1024]{3,1,2,0:T(4,128)S(1)} %all-to-all-done.2) | data formatting | bytes 3145728 | tf_op jit(solution)/shard_map/all_to_all | solution.py:106
  70.7 1.5 all-to-all-done.1
  72.2 3.6 %all-to-all-start.3 = ((f32[8,4,12,1024]{3,0,2,1:T(8,128)}), f32[8,4,12,1024]{3,0,2,1:T(8,128)S(1)}, u32[]{:S(2)}, u32[]{:S(2)}) async-start(f32[8,4,12,1024]{3,0,2,1:T(8,128)} %copy.87), calls=%async_computation.3 | async-start | bytes 3145728 | tf_op jit(solution)/shard_map/all_to_all | solution.py:105
  84.9 30.4 %all_gather.7 = f32[8,8,8]{2,1,0:T(8,128)S(1)} all-gather(f32[1,8,8]{2,1,0:T(8,128)S(1)} %add_multiply_fusion), channel_id=1, replica_groups=mesh['basin'=8,'band'=4] {'basin'}, dimensions={0}, use_global_device_ids=true | all-gather | bytes 2304 | tf_op jit(solution)/shard_map/all_gather | solution.py:10
  116.3 1.2 copy-done.2
  117.5 3.2 %all-to-all-start.5 = ((s32[4,1,4]{2,1,0:T(1,128)}), s32[4,1,4]{2,1,0:T(1,128)S(1)}, u32[]{:S(2)}, u32[]{:S(2)}) async-start(s32[4,1,4]{2,1,0:T(1,128)} %bitcast.45), calls=%async_computation.5 | async-start | bytes 4096 | tf_op jit(solution)/shard_map/all_to_all | solution.py:154
  120.7 2.4 %copy.88 = f32[8,4,12,1024]{3,2,1,0:T(8,128)S(1)} copy(f32[8,4,12,1024]{3,0,2,1:T(8,128)} %copy-done.2) | data formatting | bytes 3145728 | tf_op jit(solution)/shard_map/all_to_all | solution.py:105
  123.0 1.3 reshape.319
  124.4 1.9 %copy.89 = f32[1024,384]{1,0:T(8,128)S(1)} copy(f32[1024,384]{0,1:T(8,128)} %bitcast.253) | data formatting | bytes 3145728 | tf_op jit(solution)/shard_map/sk,sx->kx/dot_general | solution.py:135
  129.1 1.2 scatter_custom_fusion.2
  130.2 3.3 %all-to-all-start.4 = ((f32[4,4,8]{2,1,0:T(4,128)}), f32[4,4,8]{2,1,0:T(4,128)S(1)}, u32[]{:S(2)}, u32[]{:S(2)}) async-start(f32[4,4,8]{2,1,0:T(4,128)} %bitcast.43), calls=%async_computation.4 | async-start | bytes 16384 | tf_op jit(solution)/shard_map/all_to_all | solution.py:147
  136.0 1.3 all-to-all-done.4
  138.2 19.5 %all-reduce = f32[64]{0:T(128)S(1)} all-reduce(f32[64]{0:T(128)S(1)} %dynamic-update-slice), channel_id=2, replica_groups=mesh['basin'=8,'band'=4] {'basin'}, use_global_device_ids=true, to_apply=%add | all-reduce | flops 64 | bytes 512
  157.8 2.0 %while.16 = (s32[]{:T(128)}, f32[8,8]{1,0:T(8,128)S(1)}, f32[8]{0:T(128)S(1)}, s32[]{:T(128)}, f32[8,8,8]{2,1,0:T(8,128)S(1)}, /*index=5*/f32[8,8]{1,0:T(8,128)S(1)}, s32[]{:T(128)}, s32[]{:T(128)}) while((s32[]{:T(128)}, f32[8,8]{1,0:T(8,128)S(1)}, f32[8]{0:T(128)S(1)}, s32[]{:T(128)}, f32[8,8,8]{2,1,0:T(8,128)S(1)}, ...), condition=%wide.region_7.8_spmd.clone, body=%wide.region_6.7_spmd.clone.sunk | while | flops 7012 | bytes 21460 | solution.py:19
  (114 shorter events, 15.4 us)
Async XLA Ops:
  0.6 126.5 %copy-start = (f32[8,128,128]{2,1,0:T(8,128)S(1)}, f32[8,128,128]{2,1,0:T(8,128)}, u32[]{:S(2)}) copy-start(f32[8,128,128]{2,1,0:T(8,128)} %param.23) | copy-start | bytes 1572868
  0.6 15.2 %copy-start.1 = (f32[192,128]{1,0:T(8,128)S(1)}, f32[192,128]{1,0:T(8,128)}, u32[]{:S(2)}) copy-start(f32[192,128]{1,0:T(8,128)} %param.19) | copy-start | bytes 294916
  0.7 15.2 %copy-start.4 = (f32[192,128]{1,0:T(8,128)S(1)}, f32[192,128]{1,0:T(8,128)}, u32[]{:S(2)}) copy-start(f32[192,128]{1,0:T(8,128)} %param.18) | copy-start | bytes 294916
  0.7 15.2 %copy-start.3 = (f32[192,128]{1,0:T(8,128)S(1)}, f32[192,128]{1,0:T(8,128)}, u32[]{:S(2)}) copy-start(f32[192,128]{1,0:T(8,128)} %param.20) | copy-start | bytes 294916
  4.4 18.1 %all-to-all-start = ((s32[8,4,12]{2,1,0:T(4,128)}), s32[8,4,12]{2,1,0:T(4,128)S(1)}, u32[]{:S(2)}, u32[]{:S(2)}) async-start(s32[8,4,12]{2,1,0:T(4,128)} %reshape.315), calls=%async_computation | async-start | bytes 32768 | tf_op jit(solution)/shard_map/all_to_all | solution.py:116
  22.5 45.8 %copy-start.10 = (s32[8]{0:T(128)S(1)}, s32[8]{0:T(128)}, u32[]{:S(2)}) copy-start(s32[8]{0:T(128)} %param.26) | copy-start | bytes 100
  22.5 42.6 %all-to-all-start.2 = ((f32[8,4,12,1024]{3,1,2,0:T(4,128)}), f32[8,4,12,1024]{3,1,2,0:T(4,128)S(1)}, u32[]{:S(2)}, u32[]{:S(2)}) async-start(f32[8,4,12,1024]{3,1,2,0:T(4,128)} %copy.86), calls=%async_computation.2 | async-start | bytes 3145728 | tf_op jit(solution)/shard_map/all_to_all | solution.py:106
  65.1 7.1 %all-to-all-start.1 = ((s32[4,8,1,12]{3,1,2,0:T(8,128)}), s32[4,8,1,12]{3,1,2,0:T(8,128)S(1)}, u32[]{:S(2)}, u32[]{:S(2)}) async-start(s32[4,8,1,12]{3,1,2,0:T(8,128)} %pad_add_fusion), calls=%async_computation.1 | async-start | bytes 32768 | tf_op jit(solution)/shard_map/all_to_all | solution.py:113
  70.7 6.5 %copy-start.5 = (f32[1,1,128,128]{3,2,1,0:T(8,128)S(1)}, f32[1,1,128,128]{3,2,1,0:T(8,128)}, u32[]{:S(2)}) copy-start(f32[1,1,128,128]{3,2,1,0:T(8,128)} %param.28) | copy-start | bytes 196612
  70.7 7.1 %copy-start.8 = (f32[1,1,128]{2,1,0:T(1,128)S(1)}, f32[1,1,128]{2,1,0:T(1,128)}, u32[]{:S(2)}) copy-start(f32[1,1,128]{2,1,0:T(1,128)} %param.29) | copy-start | bytes 1540
  72.2 44.1 %all-to-all-start.3 = ((f32[8,4,12,1024]{3,0,2,1:T(8,128)}), f32[8,4,12,1024]{3,0,2,1:T(8,128)S(1)}, u32[]{:S(2)}, u32[]{:S(2)}) async-start(f32[8,4,12,1024]{3,0,2,1:T(8,128)} %copy.87), calls=%async_computation.3 | async-start | bytes 3145728 | tf_op jit(solution)/shard_map/all_to_all | solution.py:105
  116.3 1.2 copy-start.2
  117.5 12.8 %all-to-all-start.5 = ((s32[4,1,4]{2,1,0:T(1,128)}), s32[4,1,4]{2,1,0:T(1,128)S(1)}, u32[]{:S(2)}, u32[]{:S(2)}) async-start(s32[4,1,4]{2,1,0:T(1,128)} %bitcast.45), calls=%async_computation.5 | async-start | bytes 4096 | tf_op jit(solution)/shard_map/all_to_all | solution.py:154
  126.3 1.9 %copy-start.6 = (f32[8,128]{1,0:T(8,128)S(1)}, f32[8,128]{1,0:T(8,128)}, u32[]{:S(2)}) copy-start(f32[8,128]{1,0:T(8,128)} %param.24) | copy-start | bytes 12292
  126.3 1.9 %copy-start.7 = (f32[8,128]{1,0:T(8,128)S(1)}, f32[8,128]{1,0:T(8,128)}, u32[]{:S(2)}) copy-start(f32[8,128]{1,0:T(8,128)} %param.25) | copy-start | bytes 12292
  126.3 7.2 %copy-start.12 = (u32[32]{0:T(128)S(1)}, u32[32]{0:T(128)}, u32[]{:S(2)}) copy-start(u32[32]{0:T(128)} %constant.83) | copy-start | bytes 388
  126.3 11.4 %copy-start.9 = (f32[1,1,128]{2,1,0:T(1,128)S(1)}, f32[1,1,128]{2,1,0:T(1,128)}, u32[]{:S(2)}) copy-start(f32[1,1,128]{2,1,0:T(1,128)} %param.30) | copy-start | bytes 1540
  126.3 33.5 %copy-start.11 = (f32[1,8]{1,0:T(1,128)S(1)}, f32[1,8]{1,0:T(1,128)}, u32[]{:S(2)}) copy-start(f32[1,8]{1,0:T(1,128)} %param.31) | copy-start | bytes 100
  130.2 7.1 %all-to-all-start.4 = ((f32[4,4,8]{2,1,0:T(4,128)}), f32[4,4,8]{2,1,0:T(4,128)S(1)}, u32[]{:S(2)}, u32[]{:S(2)}) async-start(f32[4,4,8]{2,1,0:T(4,128)} %bitcast.43), calls=%async_computation.4 | async-start | bytes 16384 | tf_op jit(solution)/shard_map/all_to_all | solution.py:147
